TPU v7x, 256 devices: a whole 4x4x8 slice. The times are simulated.
256 devices in a mesh: dp: 2 (over y_hi), retr: 16 (over x, y_lo, core), tensor: 8 (over z).
Axes of the slice: x: 4, y: 4 (y_hi: 2, y_lo: 2; y = y_hi * 2 + y_lo), z: 8, core: 2. Of those that a mesh axis runs over, the one named last changes fastest.
Arguments:
- hidden_in: bfloat16 [16384, 4096], P(('dp', 'retr'), 'tensor'), may hold values from -12 to 12
- norm_gain: float32 [4096], replicated, may hold values from 0.1 to 1.9
- nbr_table: int32 [256, 2], P(('dp', 'retr')), may hold values from 0 to 63, as said below
- encodings: bfloat16 [64, 128, 1024], P('retr'), may hold values from -21 to 21
- enc_mask: int32 [64, 4], P('retr'), may hold values from 0 to 1, as said below
- w_query: bfloat16 [4096, 4096], P(None, 'tensor'), may hold values from -0.02703125 to 0.02703125
- w_key: bfloat16 [1024, 4096], P(None, 'tensor'), may hold values from -0.1021875 to 0.1021875
- w_value: bfloat16 [1024, 4096], P(None, 'tensor'), may hold values from -0.1875 to 0.1875
- w_out: bfloat16 [4096, 4096], P('tensor'), may hold values from -0.125 to 0.125
Outputs:
- mixed: bfloat16 [16384, 4096], P(('dp', 'retr'), 'tensor')
Inputs may be any that keep to these rules, and one draw needn't show every extreme that they name: `nbr_table`: each aligned block of 8 table rows (the rows of one device) holds 16 distinct ids; at most 2 of them share the value id // 4, and in every block some value of id // 4 has exactly 2. `enc_mask`: in each row the ones come first; the first entry is 1.
All inputs are finite; a program needn't handle non-finite values.
Results may differ from a plain program's by a relative error of at most 0.012.
The roundings to bfloat16 on the way count: a program that leaves them out, or rounds other values in their place, can miss the bound.
Values may be sent and summed in bfloat16 or wider, within the bound.
No kernel may reach another device: no remote copies, remote signals or barrier semaphores. Data moves between devices by JAX's collectives and lax.ppermute only.
A program may use at most 128 MiB of HBM per device.

v0:
```python
import math
import jax
import jax.numpy as jnp
from jax import lax
from jax.sharding import PartitionSpec as P

HD = 128
NBRS = 2
BLOCK = 32
CAP = 2


def attend_gathered(queries, key_value, selected_marks, segment_count, head_cols):
    tok_rows = queries.shape[0]
    head_count = head_cols // HD
    entry_keys = key_value.shape[0] // segment_count * key_value.shape[1]
    mask_cols = selected_marks.shape[1]
    key_block = key_value[:, :, :head_cols].reshape(segment_count, entry_keys, head_count, HD)
    value_block = key_value[:, :, head_cols:].reshape(segment_count, entry_keys, head_count, HD)
    key_live = (
        jnp.repeat(selected_marks.reshape(segment_count, NBRS * mask_cols), BLOCK, axis=1) > 0
    )
    query_block = queries.reshape(segment_count, tok_rows // segment_count, head_count, HD)
    factor = 1.0 / math.sqrt(HD)
    scores = (
        jnp.einsum("cqhd,ckhd->chqk", query_block, key_block, preferred_element_type=jnp.float32)
        * factor
    )
    key_open = key_live[:, None, None, :]
    scores = jnp.where(key_open, scores, -1e30)
    row_max = jnp.max(scores, axis=-1, keepdims=True)
    weights = jnp.exp(scores - row_max) * key_open.astype(jnp.float32)
    probabilities = (weights / jnp.sum(weights, axis=-1, keepdims=True)).astype(jnp.bfloat16)
    attended = jnp.einsum(
        "chqk,ckhd->cqhd", probabilities, value_block, preferred_element_type=jnp.float32
    )
    return attended.astype(jnp.bfloat16).reshape(tok_rows, head_cols)


def local(hidden_in, norm_gain, nbr_table, encodings, enc_mask, w_query, w_key, w_value, w_out):
    segment_count = nbr_table.shape[0]
    nb_dev, entry_len, enc_width = encodings.shape
    mask_cols = enc_mask.shape[1]
    head_cols = w_key.shape[1]
    wanted = nbr_table.reshape(-1)
    need_count = wanted.shape[0]
    info = jnp.concatenate([wanted, enc_mask.reshape(-1)])
    all_info = lax.all_gather(info, "retr", axis=0, tiled=False)
    retr_count = all_info.shape[0]
    all_wanted = all_info[:, :need_count]
    all_marks = all_info[:, need_count:].reshape(retr_count * nb_dev, mask_cols)
    gathered = lax.all_gather(hidden_in, "tensor", axis=1, tiled=True)
    w_both = jnp.concatenate([w_key, w_value], axis=1)
    own_kv = (
        jnp.dot(
            encodings.reshape(nb_dev * entry_len, enc_width),
            w_both,
            preferred_element_type=jnp.float32,
        )
        .astype(jnp.bfloat16)
        .reshape(nb_dev, entry_len * 2 * head_cols)
    )
    me = lax.axis_index("retr")
    mine = all_wanted // nb_dev == me
    rank = jnp.cumsum(mine.astype(jnp.int32), axis=1) - 1
    slot_ids = jnp.arange(CAP, dtype=jnp.int32)
    chosen = mine[:, None, :] & (rank[:, None, :] == slot_ids[None, :, None])
    local_idx = jnp.sum(jnp.where(chosen, all_wanted[:, None, :] % nb_dev, 0), axis=2)
    pick = (local_idx[:, :, None] == jnp.arange(nb_dev, dtype=jnp.int32)).astype(jnp.bfloat16)
    send = jnp.einsum("qjn,nf->qjf", pick, own_kv, preferred_element_type=jnp.float32).astype(
        jnp.bfloat16
    )
    recv = lax.all_to_all(send, "retr", 0, 0, tiled=True)
    owner = wanted // nb_dev
    same = owner[:, None] == owner[None, :]
    earlier = jnp.arange(need_count)[None, :] < jnp.arange(need_count)[:, None]
    my_rank = jnp.sum((same & earlier).astype(jnp.int32), axis=1)
    flat_idx = owner * CAP + my_rank
    key_value = jnp.take(recv.reshape(retr_count * CAP, -1), flat_idx, axis=0)
    key_value = key_value.reshape(need_count, entry_len, 2 * head_cols)
    picked_marks = jnp.take(all_marks, wanted, axis=0)
    widened = gathered.astype(jnp.float32)
    mean_sq = jnp.mean(widened * widened, axis=-1, keepdims=True)
    normed = (widened * lax.rsqrt(mean_sq + 1e-05) * norm_gain).astype(jnp.bfloat16)
    queries = jnp.dot(normed, w_query, preferred_element_type=jnp.float32).astype(jnp.bfloat16)
    attended = attend_gathered(queries, key_value, picked_marks, segment_count, head_cols)
    partial_value = jnp.dot(attended, w_out, preferred_element_type=jnp.float32)
    summed = lax.psum_scatter(
        partial_value.astype(jnp.bfloat16), "tensor", scatter_dimension=1, tiled=True
    )
    return (hidden_in.astype(jnp.float32) + summed.astype(jnp.float32)).astype(jnp.bfloat16)


def solution(mesh):
    in_specs = (
        P(("dp", "retr"), "tensor"),
        P(),
        P(("dp", "retr"), None),
        P("retr", None, None),
        P("retr", None),
        P(None, "tensor"),
        P(None, "tensor"),
        P(None, "tensor"),
        P("tensor", None),
    )
    out_specs = P(("dp", "retr"), "tensor")
    return jax.shard_map(local, mesh=mesh, in_specs=in_specs, out_specs=out_specs, check_vma=False)
```

profile of v0, /device:TPU:1, one launch (start us, length us, event | category | flops | bytes accessed | tf_op | source)
XLA Modules:
  0.0 317.1 jit_solution(4664920492474158840)
XLA Ops:
  6.5 0.7 all-gather.3.cloned.1.call-update
  7.3 0.8 copy.37
  8.0 0.1 reshape.243
  8.1 0.8 reshape.244
  8.9 1.3 dynamic-slice
  10.8 0.2 add_dynamic-update-slice_fusion
  11.0 10.8 %all-reduce = s32[512]{0:T(512)S(1)} all-reduce(s32[512]{0:T(512)S(1)} %add_dynamic-update-slice_fusion), channel_id=2, replica_groups=mesh['dp'=2,'retr'=16,'tensor'=8] {'retr'}, use_global_device_ids=true, to_apply=%add | all-reduce | flops 512 | bytes 4096
  21.8 0.1 reshape.278
  21.9 2.8 fusion.20
  24.7 0.2 reduce_window_sum.11
  24.9 0.5 copy.38
  25.4 0.8 reshape.284
  26.2 0.1 fusion.54
  26.3 0.1 select_reduce_fusion
  26.4 3.0 convolution_convert_fusion
  29.4 16.4 %copy.39 = bf16[16,2,131072]{2,1,0:T(2,128)(2,1)} copy(bf16[16,2,131072]{2,0,1:T(8,128)(2,1)S(1)} %convolution_convert_fusion) | data formatting | bytes 16777216 | tf_op jit(solution)/shard_map/convert_element_type | solution.py:70
  45.7 7.8 %all-to-all-start = ((bf16[16,2,131072]{2,1,0:T(2,128)(2,1)}), bf16[16,2,131072]{2,1,0:T(2,128)(2,1)}, u32[]{:S(2)}, u32[]{:S(2)}) async-start(bf16[16,2,131072]{2,1,0:T(2,128)(2,1)} %copy.39), calls=%async_computation | async-start | bytes 16777216 | tf_op jit(solution)/shard_map/all_to_all | solution.py:73
  53.5 0.1 reshape.248
  53.7 0.2 convert_reduce_fusion
  53.9 0.6 gather_fusion
  54.5 0.1 gather.15
  54.6 0.1 copy.42
  54.7 0.1 copy.43
  54.8 0.1 broadcast_in_dim.71
  54.8 0.1 gt.19
  55.0 12.6 %all-gather.3.cloned.1.call-done = bf16[512,4096]{1,0:T(8,128)(2,1)} async-done(((bf16[512,512]{1,0:T(8,128)(2,1)}), bf16[512,4096]{1,0:T(8,128)(2,1)}) %all-gather.3.cloned.1.call-update) | async-done | bytes 4194320 | tf_op jit(solution)/shard_map/all_gather | solution.py:52
  67.5 3.2 %fusion.1 = f32[512]{0:T(512)S(1)} fusion(bf16[512,4096]{1,0:T(8,128)(2,1)} %all-gather.3.cloned.1.call-done), kind=kLoop, calls=%fused_computation.7 | loop fusion | flops 6290944 | bytes 4196352 | tf_op jit(solution)/shard_map/reduce_sum | solution.py:83
  70.8 0.2 copy-done.2
  71.0 4.6 %fusion.26 = bf16[512,512]{1,0:T(8,128)(2,1)S(1)} fusion(bf16[4096,512]{1,0:T(8,128)(2,1)} %param.14, bf16[512,4096]{1,0:T(8,128)(2,1)S(1)} %copy-done.2, f32[4096]{0:T(1024)S(1)} %copy-done.7, f32[512]{0:T(512)S(1)} %add_rsqrt_fusion), kind=kOutput, calls=%fused_computation.31 | convolution fusion | flops 2156134400 | bytes 8931328 | tf_op jit(solution)/shard_map/dot_general | solution.py:85
  75.6 0.1 reshape.251
  75.7 108.4 %all-to-all-done = bf16[16,2,131072]{2,1,0:T(2,128)(2,1)} async-done(((bf16[16,2,131072]{2,1,0:T(2,128)(2,1)}), bf16[16,2,131072]{2,1,0:T(2,128)(2,1)}, u32[]{:S(2)}, u32[]{:S(2)}) %all-to-all-start) | async-done | bytes 8388640 | tf_op jit(solution)/shard_map/all_to_all | solution.py:73
  184.0 8.4 %reshape.247 = bf16[32,131072]{1,0:T(8,128)(2,1)} reshape(bf16[16,2,131072]{2,1,0:T(2,128)(2,1)} %all-to-all-done) | data formatting | bytes 16777216 | tf_op jit(solution)/shard_map/reshape | solution.py:79
  192.5 5.7 %fusion.52 = (bf16[32,65536]{1,0:T(8,128)(2,1)}, bf16[32,65536]{1,0:T(8,128)(2,1)}) fusion(bf16[32,131072]{1,0:T(8,128)(2,1)} %reshape.247), kind=kLoop, calls=%fused_computation.86 | loop fusion | bytes 16777216 | tf_op jit(solution)/shard_map/jit(_take)/gather | solution.py:79
  198.2 6.4 %gather_fusion.1 = bf16[16,65536]{1,0:T(8,128)(2,1)S(1)} fusion(bf16[32,65536]{1,0:T(8,128)(2,1)} %get-tuple-element.8, s32[1024]{0:T(1024)S(1)} %get-tuple-element.19), kind=kCustom, calls=%fused_computation.1 | custom fusion | bytes 4194368 | tf_op jit(solution)/shard_map/jit(_take)/gather | solution.py:79
  204.5 7.7 %gather_fusion.2 = bf16[16,65536]{1,0:T(8,128)(2,1)} fusion(bf16[32,65536]{1,0:T(8,128)(2,1)} %get-tuple-element.9, s32[1024]{0:T(1024)S(1)} %get-tuple-element.19), kind=kCustom, calls=%fused_computation.2 | custom fusion | bytes 4194368 | tf_op jit(solution)/shard_map/jit(_take)/gather | solution.py:79
  212.2 1.9 pad_maximum_fusion
  214.1 4.2 %copy.48 = bf16[2,8,128,1024]{3,2,1,0:T(8,128)(2,1)} copy(bf16[2,8,128,1024]{3,1,2,0:T(8,128)(2,1)S(1)} %bitcast.31) | data formatting | bytes 8388608
  218.3 6.9 %copy.41 = bf16[16,128,1024]{1,0,2:T(8,128)(2,1)} copy(bf16[16,128,1024]{2,1,0:T(8,128)(2,1)} %bitcast.32) | data formatting | bytes 8388608 | tf_op jit(solution)/shard_map/jit(_take)/gather | solution.py:79
  225.2 2.6 broadcast_select_fusion
  227.9 2.0 fusion.53
  229.9 4.1 %reshape.252 = bf16[8,256,4,128]{1,0,3,2:T(8,128)(2,1)} reshape(bf16[16,128,512]{1,0,2:T(8,128)(2,1)} %get-tuple-element.10) | data formatting | bytes 4194304 | tf_op jit(solution)/shard_map/reshape | solution.py:18
  233.9 2.2 reshape.249
  236.1 4.4 %fusion.55 = (f32[8,4,64]{2,1,0:T(4,128)S(1)}, f32[8,4,64,256]{3,2,1,0:T(8,128)}) fusion(f32[8,256]{1,0:T(8,128)S(1)} %convert_element_type.63, pred[8,256]{1,0:T(8,128)(4,1)S(1)} %gt.19, bf16[8,256,4,128]{1,0,3,2:T(8,128)(2,1)} %reshape.252, bf16[8,64,4,128]{3,2,1,0:T(4,128)(2,1)S(1)} %reshape.251), kind=kOutput, calls=%fused_computation.89 | convolution fusion | flops 136839424 | bytes 4737024 | tf_op jit(solution)/shard_map/sub | solution.py:32
  240.5 2.6 fusion.29
  243.2 0.4 copy.47
  243.6 4.3 %convolution_convert_fusion.1 = bf16[512,4096]{1,0:T(8,128)(2,1)} fusion(bf16[512,4096]{1,0:T(8,128)(2,1)S(1)} %copy-done.6, bf16[64,8,4,128]{3,2,1,0:T(4,128)(2,1)S(1)} %bitcast.33), kind=kOutput, calls=%fused_computation.10 | convolution fusion | flops 2149580800 | bytes 8912896 | tf_op jit(solution)/shard_map/dot_general | solution.py:87
  247.9 60.3 %reduce-scatter.2.cloned.1.call-done = bf16[512,512]{1,0:T(8,128)(2,1)} async-done(((bf16[512,4096]{1,0:T(8,128)(2,1)}), bf16[512,512]{1,0:T(8,128)(2,1)}) %reduce-scatter.2.cloned.1.call-update) | async-done | bytes 524304 | tf_op jit(solution)/shard_map/reduce_scatter | solution.py:88
  308.2 2.0 add_convert_fusion
  (30 shorter events, 0.3 us)
Async XLA Ops:
  6.5 15.3 %copy-start = (bf16[4,128,1024]{2,1,0:T(8,128)(2,1)S(1)}, bf16[4,128,1024]{2,1,0:T(8,128)(2,1)}, u32[]{:S(2)}) copy-start(bf16[4,128,1024]{2,1,0:T(8,128)(2,1)} %param.12) | copy-start | bytes 3145732
  6.5 61.0 %all-gather.3.cloned.1.call-start = ((), (), s32[]{:S(2)}) async-start(), calls=%async_computation.2 | async-start | bytes 4718592 | tf_op jit(solution)/shard_map/all_gather | solution.py:52
  45.7 8.9 %copy-start.5 = (s32[8,2]{0,1:T(2,128)S(1)}, s32[8,2]{0,1:T(2,128)}, u32[]{:S(2)}) copy-start(s32[8,2]{0,1:T(2,128)} %param.11) | copy-start | bytes 196
  45.7 138.3 %all-to-all-start = ((bf16[16,2,131072]{2,1,0:T(2,128)(2,1)}), bf16[16,2,131072]{2,1,0:T(2,128)(2,1)}, u32[]{:S(2)}, u32[]{:S(2)}) async-start(bf16[16,2,131072]{2,1,0:T(2,128)(2,1)} %copy.39), calls=%async_computation | async-start | bytes 16777216 | tf_op jit(solution)/shard_map/all_to_all | solution.py:73
  53.5 17.3 %copy-start.7 = (f32[4096]{0:T(1024)S(1)}, f32[4096]{0:T(1024)}, u32[]{:S(2)}) copy-start(f32[4096]{0:T(1024)} %param.10) | copy-start | bytes 49156
  53.5 254.8 %reduce-scatter.2.cloned.1.call-start = ((), (), s32[]{:S(2)}) async-start(), calls=%async_computation.3 | async-start | bytes 4718592 | tf_op jit(solution)/shard_map/reduce_scatter | solution.py:88
  67.5 3.4 %copy-start.2 = (bf16[512,4096]{1,0:T(8,128)(2,1)S(1)}, bf16[512,4096]{1,0:T(8,128)(2,1)}, u32[]{:S(2)}) copy-start(bf16[512,4096]{1,0:T(8,128)(2,1)} %all-gather.3.cloned.1.call-done) | copy-start | bytes 12582916
  236.1 4.4 %copy-start.4 = (bf16[8,256,4,128]{1,0,3,2:T(8,128)(2,1)S(1)}, bf16[8,256,4,128]{1,0,3,2:T(8,128)(2,1)}, u32[]{:S(2)}) copy-start(bf16[8,256,4,128]{1,0,3,2:T(8,128)(2,1)} %reshape.249) | copy-start | bytes 6291460
  240.5 3.1 copy-start.6
  243.6 66.6 %copy-start.1 = (bf16[4,128,1024]{2,1,0:T(8,128)(2,1)S(1)}, bf16[4,128,1024]{2,1,0:T(8,128)(2,1)}, u32[]{:S(2)}) copy-start(bf16[4,128,1024]{2,1,0:T(8,128)(2,1)} %param.12) | copy-start | bytes 3145732
  247.9 60.4 %copy-start.3 = (bf16[512,512]{1,0:T(8,128)(2,1)S(1)}, bf16[512,512]{1,0:T(8,128)(2,1)}, u32[]{:S(2)}) copy-start(bf16[512,512]{1,0:T(8,128)(2,1)} %param.9) | copy-start | bytes 1572868
Sparse Core Ops, SparseCore 0:
  9.1 58.3 all-gather.2
  248.0 60.1 reduce-scatter.1
where the time goes:
time: 318 us; the launch traced here: 317 us
  waiting for transfers between devices  182 us (57%)
  local copies, waits for them, and re-layouts  70 us (22%)
  matrix products  21.7 us (7%)
  between operations  14.2 us (4%)
  blocking collectives  10.8 us (3%)
  other arithmetic  10.5 us (3%)
  starting transfers between devices  7.8 us (2%)
    all_to_all x1, waiting for transfers between devices, local(): recv = lax.all_to_all(send, 'retr', 0, 0, tiled=True)  108 us
    reduce_scatter x1, waiting for transfers between devices, local(): lax.psum_scatter(partial_value.astype(jnp.bfloat16), 'tensor', scatter_di...  60.3 us
    gather x4, local copies, waits for them, and re-layouts, local(): key_value = jnp.take(recv.reshape(retr_count * CAP, -1), flat_idx, axis=0)  26.6 us
    convert_element_type x1, local copies, waits for them, and re-layouts, local(): jnp.einsum('qjn,nf->qjf', pick, own_kv, preferred_element_type=jnp.float32)  16.4 us
    all_gather x1, waiting for transfers between devices, local(): gathered = lax.all_gather(hidden_in, 'tensor', axis=1, tiled=True)  12.6 us
    unnamed x1, blocking collectives  10.8 us
    reshape x1, local copies, waits for them, and re-layouts, local(): key_value = jnp.take(recv.reshape(retr_count * CAP, -1), flat_idx, axis=0)  8.44 us
    all_to_all x1, starting transfers between devices, local(): recv = lax.all_to_all(send, 'retr', 0, 0, tiled=True)  7.76 us
  transfers between devices with their start and end apart: 3, of which 3 were waited for; matrix products, arithmetic and copies ran while one was open for 11% of the time, Pallas kernels for 0%

commit v1 on v0

--- a/solution.py
+++ b/solution.py
@@ -49,7 +49,8 @@
     retr_count = all_info.shape[0]
     all_wanted = all_info[:, :need_count]
     all_marks = all_info[:, need_count:].reshape(retr_count * nb_dev, mask_cols)
-    gathered = lax.all_gather(hidden_in, "tensor", axis=1, tiled=True)
+    sent = jnp.stack([hidden_in] * lax.axis_size("tensor"))
+    gathered = jnp.concatenate(lax.all_to_all(sent, "tensor", 0, 0), axis=1)
     w_both = jnp.concatenate([w_key, w_value], axis=1)
     own_kv = (
         jnp.dot(

time: 318 us -> 379 us (1.19)
  waiting for transfers between devices: 182 us -> 233 us
  starting transfers between devices: 7.8 us -> 15 us
    all_to_all x0 -> x1, waiting for transfers between devices: none -> 59.7 us  [local(): gathered = jnp.concatenate(lax.all_to_all(sent, 'tensor', 0, 0), axis=1)]
    all_to_all x1, waiting for transfers between devices: 108 us -> 121 us  [local(): recv = lax.all_to_all(send, 'retr', 0, 0, tiled=True)]
    all_gather x1 -> x0, waiting for transfers between devices: 12.6 us -> none  [local(): gathered = lax.all_gather(hidden_in, 'tensor', axis=1, tiled=True)]
    all_to_all x0 -> x1, starting transfers between devices: none -> 9.13 us  [local(): gathered = jnp.concatenate(lax.all_to_all(sent, 'tensor', 0, 0), axis=1)]
    reduce_scatter x1, waiting for transfers between devices: 60.3 us -> 52.3 us  [local(): lax.psum_scatter(partial_value.astype(jnp.bfloat16), 'tensor', scatter_di...]
  transfers between devices with their start and end apart: 3 -> 3, of which waited for: 3 -> 3; matrix products, arithmetic and copies ran while one was open for 11% -> 9% of each run, Pallas kernels for 0% -> 0%
where the time goes in v1:
time: 379 us
  waiting for transfers between devices  233 us (61%)
  local copies, waits for them, and re-layouts  72 us (19%)
  matrix products  19.5 us (5%)
  starting transfers between devices  15 us (4%)
  between operations  14.2 us (4%)
  other arithmetic  13.3 us (4%)
  blocking collectives  11.5 us (3%)
    all_to_all x1, waiting for transfers between devices, local(): recv = lax.all_to_all(send, 'retr', 0, 0, tiled=True)  121 us
    all_to_all x1, waiting for transfers between devices, local(): gathered = jnp.concatenate(lax.all_to_all(sent, 'tensor', 0, 0), axis=1)  59.7 us
    reduce_scatter x1, waiting for transfers between devices, local(): lax.psum_scatter(partial_value.astype(jnp.bfloat16), 'tensor', scatter_di...  52.3 us
    gather x4, local copies, waits for them, and re-layouts, local(): key_value = jnp.take(recv.reshape(retr_count * CAP, -1), flat_idx, axis=0)  26.6 us
    convert_element_type x1, local copies, waits for them, and re-layouts, local(): jnp.einsum('qjn,nf->qjf', pick, own_kv, preferred_element_type=jnp.float32)  16.4 us
    unnamed x1, blocking collectives  11.5 us
    all_to_all x1, starting transfers between devices, local(): gathered = jnp.concatenate(lax.all_to_all(sent, 'tensor', 0, 0), axis=1)  9.13 us
    reshape x1, local copies, waits for them, and re-layouts, local(): key_value = jnp.take(recv.reshape(retr_count * CAP, -1), flat_idx, axis=0)  8.43 us
  transfers between devices with their start and end apart: 3, of which 3 were waited for; matrix products, arithmetic and copies ran while one was open for 9% of the time, Pallas kernels for 0%

profile of v1, /device:TPU:1, one launch (start us, length us, event | category | flops | bytes accessed | tf_op | source)
XLA Modules:
  0.0 378.5 jit_solution(1549500198755615997)
XLA Ops:
  6.5 1.3 copy.46
  7.9 2.3 stack.2
  10.2 9.1 %all-to-all-start.1 = ((bf16[8,512,512]{1,2,0:T(8,128)(2,1)}), bf16[8,512,512]{1,2,0:T(8,128)(2,1)}, u32[]{:S(2)}, u32[]{:S(2)}) async-start(bf16[8,512,512]{1,2,0:T(8,128)(2,1)} %stack.2), calls=%async_computation.1 | async-start | bytes 8388608 | tf_op jit(solution)/shard_map/all_to_all | solution.py:53
  19.3 0.1 copy.39
  19.4 0.1 reshape.249
  19.5 0.1 reshape.250
  19.6 0.6 dynamic-slice
  20.8 0.2 add_dynamic-update-slice_fusion
  21.0 11.5 %all-reduce = s32[512]{0:T(512)S(1)} all-reduce(s32[512]{0:T(512)S(1)} %add_dynamic-update-slice_fusion), channel_id=2, replica_groups=mesh['dp'=2,'retr'=16,'tensor'=8] {'retr'}, use_global_device_ids=true, to_apply=%add | all-reduce | flops 512 | bytes 4096
  32.5 0.1 reshape.285
  32.6 0.2 reduce_window_sum.11
  32.7 2.8 fusion.15
  35.6 0.5 copy.40
  36.1 0.8 reshape.291
  37.0 0.1 select_reduce_fusion
  37.1 3.0 convolution_convert_fusion
  40.1 16.4 %copy.41 = bf16[16,2,131072]{2,1,0:T(2,128)(2,1)} copy(bf16[16,2,131072]{2,0,1:T(8,128)(2,1)S(1)} %convolution_convert_fusion) | data formatting | bytes 16777216 | tf_op jit(solution)/shard_map/convert_element_type | solution.py:71
  56.4 59.7 %all-to-all-done.1 = bf16[8,512,512]{1,2,0:T(8,128)(2,1)} async-done(((bf16[8,512,512]{1,2,0:T(8,128)(2,1)}), bf16[8,512,512]{1,2,0:T(8,128)(2,1)}, u32[]{:S(2)}, u32[]{:S(2)}) %all-to-all-start.1) | async-done | bytes 4194336 | tf_op jit(solution)/shard_map/all_to_all | solution.py:53
  116.2 5.8 %all-to-all-start = ((bf16[16,2,131072]{2,1,0:T(2,128)(2,1)}), bf16[16,2,131072]{2,1,0:T(2,128)(2,1)}, u32[]{:S(2)}, u32[]{:S(2)}) async-start(bf16[16,2,131072]{2,1,0:T(2,128)(2,1)} %copy.41), calls=%async_computation | async-start | bytes 16777216 | tf_op jit(solution)/shard_map/all_to_all | solution.py:74
  122.0 0.1 reshape.254
  122.2 0.2 convert_reduce_fusion
  122.4 0.6 gather_fusion
  123.2 0.1 copy.45
  123.3 0.1 broadcast_in_dim.71
  123.3 0.1 gt.19
  123.5 3.1 multiply_reduce_fusion
  126.6 2.9 fusion.2
  129.6 0.5 copy-done.7
  130.1 2.3 convolution_convert_fusion.2
  132.4 0.1 reshape.257
  132.5 121.0 %all-to-all-done = bf16[16,2,131072]{2,1,0:T(2,128)(2,1)} async-done(((bf16[16,2,131072]{2,1,0:T(2,128)(2,1)}), bf16[16,2,131072]{2,1,0:T(2,128)(2,1)}, u32[]{:S(2)}, u32[]{:S(2)}) %all-to-all-start) | async-done | bytes 8388640 | tf_op jit(solution)/shard_map/all_to_all | solution.py:74
  253.5 8.4 %reshape.253 = bf16[32,131072]{1,0:T(8,128)(2,1)} reshape(bf16[16,2,131072]{2,1,0:T(2,128)(2,1)} %all-to-all-done) | data formatting | bytes 16777216 | tf_op jit(solution)/shard_map/reshape | solution.py:80
  262.0 5.7 %fusion.44 = (bf16[32,65536]{1,0:T(8,128)(2,1)}, bf16[32,65536]{1,0:T(8,128)(2,1)}) fusion(bf16[32,131072]{1,0:T(8,128)(2,1)} %reshape.253), kind=kLoop, calls=%fused_computation.82 | loop fusion | bytes 16777216 | tf_op jit(solution)/shard_map/jit(_take)/gather | solution.py:80
  267.6 6.4 %gather_fusion.1 = bf16[16,65536]{1,0:T(8,128)(2,1)S(1)} fusion(bf16[32,65536]{1,0:T(8,128)(2,1)} %get-tuple-element.8, s32[1024]{0:T(1024)S(1)} %get-tuple-element.19), kind=kCustom, calls=%fused_computation.1 | custom fusion | bytes 4194368 | tf_op jit(solution)/shard_map/jit(_take)/gather | solution.py:80
  274.0 7.7 %gather_fusion.2 = bf16[16,65536]{1,0:T(8,128)(2,1)} fusion(bf16[32,65536]{1,0:T(8,128)(2,1)} %get-tuple-element.9, s32[1024]{0:T(1024)S(1)} %get-tuple-element.19), kind=kCustom, calls=%fused_computation.2 | custom fusion | bytes 4194368 | tf_op jit(solution)/shard_map/jit(_take)/gather | solution.py:80
  281.7 1.9 pad_maximum_fusion
  283.6 4.3 %copy.51 = bf16[2,8,128,1024]{3,2,1,0:T(8,128)(2,1)} copy(bf16[2,8,128,1024]{3,1,2,0:T(8,128)(2,1)S(1)} %bitcast.40) | data formatting | bytes 8388608
  287.8 6.9 %copy.43 = bf16[16,128,1024]{1,0,2:T(8,128)(2,1)} copy(bf16[16,128,1024]{2,1,0:T(8,128)(2,1)} %bitcast.41) | data formatting | bytes 8388608 | tf_op jit(solution)/shard_map/jit(_take)/gather | solution.py:80
  294.7 2.6 broadcast_select_fusion
  297.4 2.0 fusion.45
  299.4 4.1 %reshape.258 = bf16[8,256,4,128]{1,0,3,2:T(8,128)(2,1)} reshape(bf16[16,128,512]{1,0,2:T(8,128)(2,1)} %get-tuple-element.10) | data formatting | bytes 4194304 | tf_op jit(solution)/shard_map/reshape | solution.py:18
  303.4 2.2 reshape.255
  305.6 4.4 %fusion.47 = (f32[8,4,64]{2,1,0:T(4,128)S(1)}, f32[8,4,64,256]{3,2,1,0:T(8,128)}) fusion(f32[8,256]{1,0:T(8,128)S(1)} %convert_element_type.76, pred[8,256]{1,0:T(8,128)(4,1)S(1)} %gt.19, bf16[8,256,4,128]{1,0,3,2:T(8,128)(2,1)} %reshape.258, bf16[8,64,4,128]{3,2,1,0:T(4,128)(2,1)S(1)} %reshape.257), kind=kOutput, calls=%fused_computation.85 | convolution fusion | flops 136839424 | bytes 4737024 | tf_op jit(solution)/shard_map/sub | solution.py:32
  310.0 2.6 fusion.21
  312.7 0.4 copy.50
  313.1 4.3 %convolution_convert_fusion.1 = bf16[512,4096]{1,0:T(8,128)(2,1)} fusion(bf16[512,4096]{1,0:T(8,128)(2,1)S(1)} %copy-done.8, bf16[64,8,4,128]{3,2,1,0:T(4,128)(2,1)S(1)} %bitcast.42), kind=kOutput, calls=%fused_computation.9 | convolution fusion | flops 2149580800 | bytes 8912896 | tf_op jit(solution)/shard_map/dot_general | solution.py:88
  317.4 52.3 %reduce-scatter.2.cloned.1.call-done = bf16[512,512]{1,0:T(8,128)(2,1)} async-done(((bf16[512,4096]{1,0:T(8,128)(2,1)}), bf16[512,512]{1,0:T(8,128)(2,1)}) %reduce-scatter.2.cloned.1.call-update) | async-done | bytes 524304 | tf_op jit(solution)/shard_map/reduce_scatter | solution.py:89
  369.7 2.0 add_convert_fusion
  (36 shorter events, 0.5 us)
Async XLA Ops:
  6.5 26.2 %copy-start = (bf16[4,128,1024]{2,1,0:T(8,128)(2,1)S(1)}, bf16[4,128,1024]{2,1,0:T(8,128)(2,1)}, u32[]{:S(2)}) copy-start(bf16[4,128,1024]{2,1,0:T(8,128)(2,1)} %param.12) | copy-start | bytes 3145732
  10.2 9.1 %copy-start.6 = (s32[8,2]{0,1:T(2,128)S(1)}, s32[8,2]{0,1:T(2,128)}, u32[]{:S(2)}) copy-start(s32[8,2]{0,1:T(2,128)} %param.11) | copy-start | bytes 196
  10.2 9.3 %copy-start.5 = (s32[4,4]{1,0:T(4,128)S(1)}, s32[4,4]{1,0:T(4,128)}, u32[]{:S(2)}) copy-start(s32[4,4]{1,0:T(4,128)} %param.13) | copy-start | bytes 196
  10.2 9.4 %copy-start.9 = (u32[256]{0:T(256)S(1)}, u32[256]{0:T(256)}, u32[]{:S(2)}) copy-start(u32[256]{0:T(256)} %constant.99) | copy-start | bytes 3076
  10.2 106.0 %all-to-all-start.1 = ((bf16[8,512,512]{1,2,0:T(8,128)(2,1)}), bf16[8,512,512]{1,2,0:T(8,128)(2,1)}, u32[]{:S(2)}, u32[]{:S(2)}) async-start(bf16[8,512,512]{1,2,0:T(8,128)(2,1)} %stack.2), calls=%async_computation.1 | async-start | bytes 8388608 | tf_op jit(solution)/shard_map/all_to_all | solution.py:53
  116.2 137.4 %all-to-all-start = ((bf16[16,2,131072]{2,1,0:T(2,128)(2,1)}), bf16[16,2,131072]{2,1,0:T(2,128)(2,1)}, u32[]{:S(2)}, u32[]{:S(2)}) async-start(bf16[16,2,131072]{2,1,0:T(2,128)(2,1)} %copy.41), calls=%async_computation | async-start | bytes 16777216 | tf_op jit(solution)/shard_map/all_to_all | solution.py:74
  122.0 4.6 %copy-start.4 = (f32[4096]{0:T(1024)S(1)}, f32[4096]{0:T(1024)}, u32[]{:S(2)}) copy-start(f32[4096]{0:T(1024)} %param.10) | copy-start | bytes 49156
  122.0 247.7 %reduce-scatter.2.cloned.1.call-start = ((), (), s32[]{:S(2)}) async-start(), calls=%async_computation.3 | async-start | bytes 4718592 | tf_op jit(solution)/shard_map/reduce_scatter | solution.py:89
  126.6 3.5 copy-start.7
  305.6 4.4 %copy-start.3 = (bf16[8,256,4,128]{1,0,3,2:T(8,128)(2,1)S(1)}, bf16[8,256,4,128]{1,0,3,2:T(8,128)(2,1)}, u32[]{:S(2)}) copy-start(bf16[8,256,4,128]{1,0,3,2:T(8,128)(2,1)} %reshape.255) | copy-start | bytes 6291460
  310.0 3.1 copy-start.8
  313.1 58.6 %copy-start.1 = (bf16[4,128,1024]{2,1,0:T(8,128)(2,1)S(1)}, bf16[4,128,1024]{2,1,0:T(8,128)(2,1)}, u32[]{:S(2)}) copy-start(bf16[4,128,1024]{2,1,0:T(8,128)(2,1)} %param.12) | copy-start | bytes 3145732
  317.4 52.3 %copy-start.2 = (bf16[512,512]{1,0:T(8,128)(2,1)S(1)}, bf16[512,512]{1,0:T(8,128)(2,1)}, u32[]{:S(2)}) copy-start(bf16[512,512]{1,0:T(8,128)(2,1)} %param.9) | copy-start | bytes 1572868
Sparse Core Ops, SparseCore 0:
  317.5 52.1 reduce-scatter.1
